TPU v7x, 32 devices: a whole 2x2x4 slice. The times are simulated.
32 devices in a mesh: row: 2 (over core), col: 2 (over x), seq: 8 (over z, y).
Axes of the slice: x: 2, y: 2, z: 4, core: 2. Of those that a mesh axis runs over, the one named last changes fastest.
Arguments:
- states: bfloat16 [128, 4, 5120], P('col', None, 'row'), may hold values from -64 to 64
- norm_gain: float32 [5120], P('row'), may hold values from 0.1 to 1.9
- wq: bfloat16 [5120, 4096], P('row', 'col'), may hold values from -0.078125 to 0.078125
- wk: bfloat16 [5120, 1024], P('row', 'col'), may hold values from -0.21875 to 0.21875
- wv: bfloat16 [5120, 1024], P('row', 'col'), may hold values from -0.078125 to 0.078125
- wo: bfloat16 [4096, 5120], P('col', 'row'), may hold values from -0.09375 to 0.09375
- lengths: int32 [128], P('row'), may hold values from 1 to 8192, as said below
- slot_request: int32 [800], P(('row', 'seq')), may hold values from 0 to 64, as said below
- slot_block_number: int32 [800], P(('row', 'seq')), may hold values from 0 to 63, as said below
- paged_key_cache: bfloat16 [800, 128, 1024], P(('row', 'seq'), None, 'col'), may hold values from -120 to 120
- paged_value_cache: bfloat16 [800, 128, 1024], P(('row', 'seq'), None, 'col'), may hold values from -6 to 6
Outputs:
- attended: bfloat16 [128, 4, 5120], P('col', None, 'row')
- new_keys: bfloat16 [128, 4, 1024], P('row', None, 'col')
- new_values: bfloat16 [128, 4, 1024], P('row', None, 'col')
Inputs may be any that keep to these rules, and one draw needn't show every extreme that they name: `lengths`: within every 64 consecutive requests, 8 have exactly 8192 cached tokens and the others fewer than 128. `slot_request`: each request's block 0 and every block that holds a position visible to one of its steps stand in exactly one slot of its index of row; a long request has exactly 33 slots. 64 marks an empty slot; every index of row has empty slots. `slot_block_number`: 0 in empty slots.
All inputs are finite; a program needn't handle non-finite values.
Results may differ from a plain program's by a relative error of at most 0.034.
Values may be sent and summed in bfloat16 or wider, within the bound.
No kernel may reach another device: no remote copies, remote signals or barrier semaphores. Data moves between devices by JAX's collectives and lax.ppermute only.
A program may use at most 192 MiB of HBM per device.

v0:
```python
import math
import jax
import jax.numpy as jnp
from jax import lax
from jax.sharding import PartitionSpec as P

D = 5120
HEAD_SIZE = 128
WINDOW = 4096
SINK = 4
QUERY_PER_KEY = 4
EPSILON = 1e-05
NEGATIVE_FILL = -1e30
ROPE_BASE = 100000000.0


def rotary_apply(values, token_positions):
    half_dim = values.shape[-1] // 2
    frequency = ROPE_BASE ** (-(jnp.arange(half_dim, dtype=jnp.float32) * 2.0 / values.shape[-1]))
    angles = (token_positions.astype(jnp.float32)[..., None] * frequency)[..., None, :]
    cosine = jnp.cos(angles)
    sine_part = jnp.sin(angles)
    lower = values[..., :half_dim]
    upper = values[..., half_dim:]
    return jnp.concatenate(
        [lower * cosine - upper * sine_part, upper * cosine + lower * sine_part], -1
    )


def slot_parts(query_rows, lengths, slot_request, slot_block_number, key_rows, value_rows):
    req_count = query_rows.shape[0]
    step_count = query_rows.shape[1]
    block_len = key_rows.shape[1]
    picked = jnp.minimum(slot_request, req_count - 1)
    in_use = slot_request < req_count
    slot_queries = query_rows[picked]
    scores = jnp.einsum(
        "nsagh,nbah->nasgb", slot_queries, key_rows, preferred_element_type=jnp.float32
    ) * (1.0 / math.sqrt(HEAD_SIZE))
    key_pos = (
        slot_block_number[:, None] * block_len + jnp.arange(block_len, dtype=jnp.int32)[None, :]
    )
    own_len = lengths[picked]
    query_pos = own_len[:, None] + jnp.arange(step_count, dtype=jnp.int32)[None, :]
    visible = (
        in_use[:, None, None]
        & (key_pos[:, None, :] < own_len[:, None, None])
        & ((key_pos[:, None, :] < SINK) | (key_pos[:, None, :] > query_pos[:, :, None] - WINDOW))
    )
    visible = visible[:, None, :, None, :]
    slot_peak = jnp.max(jnp.where(visible, scores, NEGATIVE_FILL), -1)
    weights = jnp.where(visible, jnp.exp(scores - slot_peak[..., None]), 0.0)
    slot_total = jnp.sum(weights, -1)
    slot_acc = jnp.einsum(
        "nasgb,nbah->nasgh",
        weights.astype(jnp.bfloat16),
        value_rows,
        preferred_element_type=jnp.float32,
    )
    member = slot_request[None, :] == jnp.arange(req_count, dtype=jnp.int32)[:, None]
    local_peak = jnp.max(
        jnp.where(member[:, :, None, None, None], slot_peak[None], NEGATIVE_FILL), 1
    )
    return (local_peak, (slot_peak, slot_total, slot_acc, member, picked))


def pool_sums(held, running_peak):
    slot_peak, slot_total, slot_acc, member, picked = held
    factor = jnp.exp(slot_peak - running_peak[picked])
    as_member = member.astype(jnp.float32)
    running_totals = jnp.einsum(
        "rn,nasg->rasg", as_member, slot_total * factor, precision=lax.Precision.HIGHEST
    )
    weighted_values = jnp.einsum(
        "rn,nasgh->rasgh", as_member, slot_acc * factor[..., None], precision=lax.Precision.HIGHEST
    )
    return (running_totals, weighted_values)


def fresh_part(query_rows, key_all, value_all):
    step_count = query_rows.shape[1]
    used = key_all.shape[1]
    scores = jnp.einsum(
        "rsagh,ruah->rasgu", query_rows, key_all, preferred_element_type=jnp.float32
    ) * (1.0 / math.sqrt(HEAD_SIZE))
    causal = (
        jnp.arange(used, dtype=jnp.int32)[None, :]
        <= jnp.arange(step_count, dtype=jnp.int32)[:, None]
    )
    causal = causal[None, None, :, None, :]
    running_peak = jnp.max(jnp.where(causal, scores, NEGATIVE_FILL), -1)
    weights = jnp.where(causal, jnp.exp(scores - running_peak[..., None]), 0.0)
    running_totals = jnp.sum(weights, -1)
    weighted_values = jnp.einsum(
        "rasgu,ruah->rasgh",
        weights.astype(jnp.bfloat16),
        value_all,
        preferred_element_type=jnp.float32,
    )
    return (running_peak, running_totals, weighted_values)


def merge_parts(earlier, later):
    running_peak = jnp.maximum(earlier[0], later[0])
    first_factor = jnp.exp(earlier[0] - running_peak)
    second_factor = jnp.exp(later[0] - running_peak)
    running_totals = earlier[1] * first_factor + later[1] * second_factor
    weighted_values = earlier[2] * first_factor[..., None] + later[2] * second_factor[..., None]
    return (running_peak, running_totals, weighted_values)


def seq_merge(peak, total, acc, n_seq, seq_index):
    stages = n_seq.bit_length() - 1
    assert 1 << stages == n_seq
    req_count = peak.shape[0]
    per = req_count // n_seq
    rest = peak.shape[1:]
    split = [2] * stages + [per]
    stats = jnp.stack([peak, total], 0).reshape([2] + split + list(rest))
    values = acc.reshape(split + list(acc.shape[1:]))
    for bit in range(stages):
        axis = stages - 1 - bit
        mine = seq_index >> bit & 1
        pairs = [(s, s ^ 1 << bit) for s in range(n_seq)]
        keep_stats = lax.dynamic_index_in_dim(stats, mine, axis + 1, keepdims=True)
        send_stats = lax.dynamic_index_in_dim(stats, 1 - mine, axis + 1, keepdims=True)
        keep_values = lax.dynamic_index_in_dim(values, mine, axis, keepdims=True)
        send_values = lax.dynamic_index_in_dim(values, 1 - mine, axis, keepdims=True)
        got_stats = lax.ppermute(send_stats, "seq", pairs)
        got_values = lax.ppermute(send_values.astype(jnp.bfloat16), "seq", pairs).astype(
            jnp.float32
        )
        top = jnp.maximum(keep_stats[0], got_stats[0])
        keep_factor = jnp.exp(keep_stats[0] - top)
        got_factor = jnp.exp(got_stats[0] - top)
        stats = jnp.stack([top, keep_stats[1] * keep_factor + got_stats[1] * got_factor], 0)
        values = keep_values * keep_factor[..., None] + got_values * got_factor[..., None]
    stats = stats.reshape((2, per) + tuple(rest))
    values = values.reshape((per,) + tuple(acc.shape[1:]))
    return (stats[0], stats[1], values)


def on_device(
    states,
    norm_gain,
    wq,
    wk,
    wv,
    wo,
    lengths,
    slot_request,
    slot_block_number,
    paged_key_cache,
    paged_value_cache,
):
    q_width = wq.shape[1]
    k_width = wk.shape[1]
    heads_kv = k_width // HEAD_SIZE
    req_count = lengths.shape[0]
    block_len = paged_key_cache.shape[1]
    key_rows = paged_key_cache.reshape(paged_key_cache.shape[0], block_len, heads_kv, HEAD_SIZE)
    value_rows = paged_value_cache.reshape(
        paged_value_cache.shape[0], block_len, heads_kv, HEAD_SIZE
    )
    step_count = states.shape[1]
    as_float = states.astype(jnp.float32)
    squares = lax.psum(jnp.sum(as_float * as_float, -1), "row")
    normed = (as_float * lax.rsqrt(squares / D + EPSILON)[..., None] * norm_gain).astype(
        jnp.bfloat16
    )
    gathered = lax.all_gather(normed, "col", axis=0, tiled=True)
    piece_rows = gathered.reshape(req_count * lax.axis_size("row") * step_count, -1)
    parts_out = [
        jnp.dot(piece_rows, matrix, preferred_element_type=jnp.float32) for matrix in (wq, wk, wv)
    ]
    output_projected = lax.psum_scatter(
        jnp.concatenate(parts_out, axis=-1)
        .reshape(req_count * lax.axis_size("row"), step_count, -1)
        .astype(jnp.bfloat16),
        "row",
        scatter_dimension=0,
        tiled=True,
    ).astype(jnp.float32)
    token_positions = lengths[:, None] + jnp.arange(step_count, dtype=jnp.int32)[None, :]
    query_rows = rotary_apply(
        output_projected[..., :q_width].reshape(req_count, step_count, -1, HEAD_SIZE),
        token_positions,
    ).astype(jnp.bfloat16)
    query_rows = query_rows.reshape(req_count, step_count, heads_kv, QUERY_PER_KEY, HEAD_SIZE)
    current_key = rotary_apply(
        output_projected[..., q_width : q_width + k_width].reshape(
            req_count, step_count, heads_kv, HEAD_SIZE
        ),
        token_positions,
    ).astype(jnp.bfloat16)
    current_value = (
        output_projected[..., q_width + k_width :]
        .reshape(req_count, step_count, heads_kv, HEAD_SIZE)
        .astype(jnp.bfloat16)
    )
    local_peak, held = slot_parts(
        query_rows, lengths, slot_request, slot_block_number, key_rows, value_rows
    )
    local_totals, local_values = pool_sums(held, local_peak)
    n_seq = lax.axis_size("seq")
    per = req_count // n_seq
    seq_index = lax.axis_index("seq")
    mine = seq_index * per
    running_peak, running_totals, weighted_values = seq_merge(
        local_peak, local_totals, local_values, n_seq, seq_index
    )
    own_queries = lax.dynamic_slice_in_dim(query_rows, mine, per, 0)
    fresh = fresh_part(
        own_queries,
        lax.dynamic_slice_in_dim(current_key, mine, per, 0),
        lax.dynamic_slice_in_dim(current_value, mine, per, 0),
    )
    running_peak, running_totals, weighted_values = merge_parts(
        (running_peak, running_totals, weighted_values), fresh
    )
    heads_out = (
        (weighted_values / running_totals[..., None])
        .transpose(0, 2, 1, 3, 4)
        .reshape(per, step_count, -1)
        .astype(jnp.bfloat16)
    )
    piece_rows = lax.all_gather(heads_out, "row", axis=0, tiled=False)
    n_row = piece_rows.shape[0]
    product = jnp.dot(
        piece_rows.reshape(n_row * per * step_count, -1), wo, preferred_element_type=jnp.float32
    )
    partials = product.reshape(n_row, per, step_count, -1)
    own_out = lax.psum_scatter(
        partials.astype(jnp.bfloat16), "col", scatter_dimension=0, tiled=True
    ).reshape(per, step_count, -1)
    attended = lax.all_gather(own_out, "seq", axis=0, tiled=True)
    return (
        attended,
        current_key.reshape(req_count, step_count, k_width),
        current_value.reshape(req_count, step_count, k_width),
    )


def solution(mesh):
    in_specs = (
        P("col", None, "row"),
        P("row"),
        P("row", "col"),
        P("row", "col"),
        P("row", "col"),
        P("col", "row"),
        P("row"),
        P(("row", "seq")),
        P(("row", "seq")),
        P(("row", "seq"), None, "col"),
        P(("row", "seq"), None, "col"),
    )
    out_specs = (P("col", None, "row"), P("row", None, "col"), P("row", None, "col"))
    return jax.shard_map(
        on_device, mesh=mesh, in_specs=in_specs, out_specs=out_specs, check_vma=False
    )
```

profile of v0, /device:TPU:0, one launch (start us, length us, event | category | flops | bytes accessed | tf_op | source)
XLA Modules:
  0.0 265.6 jit_solution(17505629479722814669)
XLA Ops:
  7.2 2.2 fusion.9
  9.5 2.6 psum.7
  12.2 3.1 %fusion.11 = bf16[64,4,2560]{2,1,0:T(4,128)(2,1)} fusion(bf16[64,4,2560]{2,1,0:T(4,128)(2,1)} %param.11, f32[2560]{0:T(1024)} %param.12, f32[64,4]{1,0:T(8,128)S(1)} %copy.273), kind=kLoop, calls=%fused_computation.16 | loop fusion | flops 2621440 | bytes 2632704 | tf_op jit(solution)/shard_map/convert_element_type | solution.py:168
  15.4 41.7 %all-gather.4.cloned.1.call-done = bf16[128,4,2560]{2,1,0:T(4,128)(2,1)} async-done(((bf16[64,4,2560]{2,1,0:T(4,128)(2,1)}), bf16[128,4,2560]{2,1,0:T(4,128)(2,1)}) %all-gather.4.cloned.1.call-update) | async-done | bytes 2621456 | tf_op jit(solution)/shard_map/all_gather | solution.py:171
  57.1 5.3 %reshape.465 = bf16[512,2560]{1,0:T(8,128)(2,1)} reshape(bf16[128,4,2560]{2,1,0:T(4,128)(2,1)} %all-gather.4.cloned.1.call-done) | data formatting | bytes 5242880 | tf_op jit(solution)/shard_map/reshape | solution.py:172
  62.5 3.4 %convolution_convert_fusion.1 = bf16[512,512]{1,0:T(8,128)(2,1)S(1)} fusion(bf16[512,2560]{1,0:T(8,128)(2,1)} %reshape.465, bf16[2560,512]{1,0:T(8,128)(2,1)S(1)} %copy-done), kind=kOutput, calls=%fused_computation.26 | convolution fusion | flops 1342439424 | bytes 5767168 | tf_op jit(solution)/shard_map/dot_general | solution.py:174
  65.9 1.5 convolution_convert_fusion.2
  67.4 8.5 %convolution_convert_fusion = bf16[512,2048]{1,0:T(8,128)(2,1)S(1)} fusion(bf16[512,2560]{1,0:T(8,128)(2,1)S(1)} %copy-done.5, bf16[2560,2048]{1,0:T(8,128)(2,1)} %param.13), kind=kOutput, calls=%fused_computation.13 | convolution fusion | flops 5369757696 | bytes 15204352 | tf_op jit(solution)/shard_map/dot_general | solution.py:174
  75.9 1.8 pad_maximum_fusion
  77.7 6.1 %convert_element_type.83 = bf16[128,4,3072]{2,1,0:T(4,128)(2,1)} reshape(bf16[512,3072]{1,0:T(8,128)(2,1)} %pad_maximum_fusion) | data formatting | bytes 6291456 | tf_op jit(solution)/shard_map/convert_element_type | solution.py:179
  84.5 0.8 gather_fusion
  85.4 1.1 multiply_cosine_fusion
  86.5 12.4 %reshape.467 = bf16[50,128,4,128]{3,2,1,0:T(4,128)(2,1)} reshape(bf16[50,128,512]{2,1,0:T(8,128)(2,1)} %param.20) | data formatting | bytes 13107200 | tf_op jit(solution)/shard_map/reshape | solution.py:161
  98.9 12.4 %reshape.468 = bf16[50,128,4,128]{3,2,1,0:T(4,128)(2,1)} reshape(bf16[50,128,512]{2,1,0:T(8,128)(2,1)} %param.21) | data formatting | bytes 13107200 | tf_op jit(solution)/shard_map/reshape | solution.py:162
  111.2 0.6 dynamic-slice
  113.0 1.8 dynamic-slice_convert_fusion
  114.8 0.9 slice_bitcast_fusion.2
  115.8 0.8 copy-done.3
  116.6 1.5 slice.92
  118.1 2.3 reshape.509
  120.4 0.7 fusion.76
  121.2 0.6 subtract_convert_fusion
  121.7 1.4 pad_maximum_fusion.1
  123.2 0.6 copy.329
  123.7 2.2 gather_fusion.1
  125.9 7.9 %select_reduce_fusion.1 = (f32[50,4,4,4]{3,2,1,0:T(4,128)S(1)}, f32[50,4,4,4,128]{4,3,2,1,0:T(4,128)}) fusion(pred[50,4,128]{2,1,0:T(4,128)(4,1)S(1)} %or_and_fusion, bf16[50,4,4,4,128]{4,3,1,2,0:T(4,128)(2,1)} %gather_fusion.1, bf16[50,128,4,128,1]{3,2,1,0,4:T(4,128)(2,1)} %bitcast.123), kind=kOutput, calls=%fused_computation.23 | convolution fusion | flops 106083200 | bytes 9049600 | tf_op jit(solution)/shard_map/nsagh,nbah->nasgb/dot_general | solution.py:37
  133.9 1.3 select_reduce_fusion
  135.1 1.1 stack.10
  136.6 0.5 multiply_subtract_fusion
  137.4 1.2 fusion.36
  138.7 0.5 copy.303
  139.4 0.8 fusion.40
  140.2 0.8 copy_dynamic-update-slice_fusion.1
  141.0 3.2 %fusion.18 = f32[50,4,4,4]{3,2,1,0:T(4,128)S(1)} fusion(f32[50,4,4,4,128]{4,3,2,1,0:T(4,128)} %get-tuple-element.60, f32[50,4,4,4]{3,2,1,0:T(4,128)S(1)} %get-tuple-element.59, pred[50,4,128]{2,1,0:T(4,128)(4,1)S(1)} %or_and_fusion), kind=kLoop, calls=%fused_computation.33 | loop fusion | flops 1635200 | bytes 1689600 | tf_op jit(solution)/shard_map/reduce_sum | solution.py:53
  144.1 0.8 gather_fusion.2
  145.0 0.8 fusion.75
  146.8 0.8 constant_dynamic-slice_fusion.1
  147.6 1.6 collective-permute-start
  149.2 4.7 %fusion.14 = f32[50,4,4,4,128]{4,3,2,1,0:T(4,128)S(1)} fusion(bf16[50,128,4,128,1]{3,2,1,0,4:T(4,128)(2,1)} %bitcast.122, f32[50,4,4,4,128]{4,3,2,1,0:T(4,128)} %get-tuple-element.60, f32[50,4,4,4]{3,2,1,0:T(4,128)} %bitcast.135, f32[50,4,4,4]{3,2,1,0:T(4,128)S(1)} %get-tuple-element.59, pred[50,4,128]{2,1,0:T(4,128)(4,1)S(1)} %copy-done.16), kind=kOutput, calls=%fused_computation.25 | convolution fusion | flops 106905600 | bytes 9881600 | tf_op jit(solution)/shard_map/nasgb,nbah->nasgh/dot_general | solution.py:54
  153.9 2.2 fusion.12
  156.1 1.1 constant_dynamic-slice_fusion.2
  157.4 1.1 copy.308
  158.8 0.5 collective-permute-start.1
  159.3 1.1 fusion.33
  160.5 1.6 collective-permute-start.2
  162.1 1.0 fusion.28
  163.1 0.5 copy.292
  164.0 1.5 collective-permute-done.2
  165.6 2.6 collective-permute-start.4
  168.2 4.1 %collective-permute-done.1 = bf16[2,2,1,8,4,4,4,128]{7,6,5,4,3,2,1,0:T(4,128)(2,1)} collective-permute-done((bf16[2,2,1,8,4,4,4,128]{7,6,5,4,3,2,1,0:T(4,128)(2,1)S(1)}, bf16[2,2,1,8,4,4,4,128]{7,6,5,4,3,2,1,0:T(4,128)(2,1)}, u32[]{:S(2)}, u32[]{:S(2)}) %collective-permute-start.1) | collective-permute-done | bytes 524320 | tf_op jit(solution)/shard_map/ppermute | solution.py:130
  172.3 2.5 fusion.17
  174.9 1.6 collective-permute-start.3
  177.1 4.7 %collective-permute-done.3 = bf16[2,1,1,8,4,4,4,128]{7,6,5,4,3,2,1,0:T(4,128)(2,1)S(1)} collective-permute-done((bf16[2,1,1,8,4,4,4,128]{7,6,5,4,3,2,1,0:T(4,128)(2,1)S(1)}, bf16[2,1,1,8,4,4,4,128]{7,6,5,4,3,2,1,0:T(4,128)(2,1)S(1)}, u32[]{:S(2)}, u32[]{:S(2)}) %collective-permute-start.3) | collective-permute-done | bytes 262176 | tf_op jit(solution)/shard_map/ppermute | solution.py:130
  181.7 0.6 multiply_add_fusion.1
  182.4 2.5 collective-permute-start.5
  185.8 3.9 %collective-permute-done.5 = bf16[1,1,1,8,4,4,4,128]{7,6,5,4,3,2,1,0:T(4,128)(2,1)S(1)} collective-permute-done((bf16[1,1,1,8,4,4,4,128]{7,6,5,4,3,2,1,0:T(4,128)(2,1)S(1)}, bf16[1,1,1,8,4,4,4,128]{7,6,5,4,3,2,1,0:T(4,128)(2,1)S(1)}, u32[]{:S(2)}, u32[]{:S(2)}) %collective-permute-start.5) | collective-permute-done | bytes 131104 | tf_op jit(solution)/shard_map/ppermute | solution.py:130
  189.7 1.6 fusion.38
  191.5 2.0 all_gather.11
  193.5 6.6 %fusion.6 = bf16[2,8,4,2560]{3,1,2,0:T(8,128)(2,1)} fusion(bf16[2,8,4,2048]{3,1,2,0:T(8,128)(2,1)S(1)} %all_gather.11, bf16[2048,2560]{1,0:T(8,128)(2,1)} %param.16), kind=kOutput, calls=%fused_computation.9 | convolution fusion | flops 671252480 | bytes 11075584 | tf_op jit(solution)/shard_map/dot_general | solution.py:229
  200.2 11.6 %reduce-scatter.2.cloned.1.call-done = bf16[1,8,4,2560]{3,1,2,0:T(8,128)(2,1)} async-done(((bf16[2,8,4,2560]{3,1,2,0:T(8,128)(2,1)}), bf16[1,8,4,2560]{3,1,2,0:T(8,128)(2,1)}) %reduce-scatter.2.cloned.1.call-update) | async-done | bytes 163856 | tf_op jit(solution)/shard_map/reduce_scatter | solution.py:233
  211.8 1.8 slice.146
  213.6 1.1 fusion.87
  214.7 41.0 %all-gather.6.cloned.1.call-done = bf16[1,64,4,2560]{3,1,2,0:T(8,128)(2,1)} async-done(((bf16[1,8,4,2560]{3,1,2,0:T(8,128)(2,1)}), bf16[1,64,4,2560]{3,1,2,0:T(8,128)(2,1)}) %all-gather.6.cloned.1.call-update) | async-done | bytes 1310736 | tf_op jit(solution)/shard_map/all_gather | solution.py:236
  255.7 3.4 %copy.315 = bf16[64,4,2560]{2,1,0:T(4,128)(2,1)} copy(bf16[64,4,2560]{2,0,1:T(8,128)(2,1)} %bitcast.132) | data formatting | bytes 2621440
  (97 shorter events, 6.5 us)
Async XLA Ops:
  7.2 55.3 %copy-start = (bf16[2560,512]{1,0:T(8,128)(2,1)S(1)}, bf16[2560,512]{1,0:T(8,128)(2,1)}, u32[]{:S(2)}) copy-start(bf16[2560,512]{1,0:T(8,128)(2,1)} %param.15) | copy-start | bytes 7864324
  7.2 50.0 %all-gather.4.cloned.1.call-start = ((), (), s32[]{:S(2)}) async-start(), calls=%async_computation.1 | async-start | bytes 3932160 | tf_op jit(solution)/shard_map/all_gather | solution.py:171
  15.4 97.6 %all-reduce.3.cloned.1.call-start = ((), (), s32[]{:S(2)}) async-start(), calls=%async_computation.4 | async-start | bytes 6291456
  62.5 3.4 %copy-start.5 = (bf16[512,2560]{1,0:T(8,128)(2,1)S(1)}, bf16[512,2560]{1,0:T(8,128)(2,1)}, u32[]{:S(2)}) copy-start(bf16[512,2560]{1,0:T(8,128)(2,1)} %reshape.465) | copy-start | bytes 7864324
  62.5 3.4 %copy-start.18 = (bf16[2560,512]{1,0:T(8,128)(2,1)S(1)}, bf16[2560,512]{1,0:T(8,128)(2,1)}, u32[]{:S(2)}) copy-start(bf16[2560,512]{1,0:T(8,128)(2,1)} %param.14) | copy-start | bytes 7864324
  83.8 0.7 copy-start.17
  83.8 0.7 copy-start.2
  83.8 127.9 %reduce-scatter.2.cloned.1.call-start = ((), (), s32[]{:S(2)}) async-start(), calls=%async_computation.2 | async-start | bytes 491520 | tf_op jit(solution)/shard_map/reduce_scatter | solution.py:233
  98.8 12.4 %copy-start.20 = (u32[32]{0:T(128)S(1)}, u32[32]{0:T(128)}, u32[]{:S(2)}) copy-start(u32[32]{0:T(128)} %constant.92) | copy-start | bytes 388
  98.8 13.6 %copy-start.19 = (s32[50]{0:T(128)S(1)}, s32[50]{0:T(128)}, u32[]{:S(2)}) copy-start(s32[50]{0:T(128)} %param.19) | copy-start | bytes 604
  113.0 28.0 %copy-start.15 = (pred[50,4,128]{2,1,0:T(4,128)(4,1)}, pred[50,4,128]{2,1,0:T(4,128)(4,1)S(1)}, u32[]{:S(2)}) copy-start(pred[50,4,128]{2,1,0:T(4,128)(4,1)S(1)} %or_and_fusion) | copy-start | bytes 76804
  114.8 1.7 copy-start.3
  137.1 3.1 %copy-start.8 = (f32[1,2,2,2,8,4,4,4]{4,3,2,1,7,6,5,0:T(2,128)S(1)}, f32[1,2,2,2,8,4,4,4]{4,3,2,1,7,6,5,0:T(2,128)}, u32[]{:S(2)}) copy-start(f32[1,2,2,2,8,4,4,4]{4,3,2,1,7,6,5,0:T(2,128)} %stack.10) | copy-start | bytes 49156
  139.4 1.6 copy-start.11
  144.9 1.8 copy-start.6
  145.0 4.2 %copy-start.16 = (pred[50,4,128]{2,1,0:T(4,128)(4,1)S(1)}, pred[50,4,128]{2,1,0:T(4,128)(4,1)}, u32[]{:S(2)}) copy-start(pred[50,4,128]{2,1,0:T(4,128)(4,1)} %copy-done.15) | copy-start | bytes 76804
  146.8 2.4 copy-start.7
  147.6 11.7 %collective-permute-start = (f32[2,2,2,1,8,4,4,4]{4,7,6,5,2,1,3,0:T(4,128)}, f32[2,2,2,1,8,4,4,4]{4,7,6,5,2,1,3,0:T(4,128)S(1)}, u32[]{:S(2)}, u32[]{:S(2)}) collective-permute-start(f32[2,2,2,1,8,4,4,4]{4,7,6,5,2,1,3,0:T(4,128)} %constant_dynamic-slice_fusion.1), channel_id=1, source_target_pairs={{0,1},{1,0},{2,3},{3,2},{4,5},{5,4},{6,7},{7,6},{8,9},{9,8},{10,11... | collective-permute-start | bytes 49160 | tf_op jit(solution)/shard_map/ppermute | solution.py:129
  158.5 13.8 %copy-start.4 = (f32[2,2,1,8,4,4,4,128]{7,3,2,1,0,6,5,4:T(8,128)S(1)}, f32[2,2,1,8,4,4,4,128]{7,3,2,1,0,6,5,4:T(8,128)}, u32[]{:S(2)}) copy-start(f32[2,2,1,8,4,4,4,128]{7,3,2,1,0,6,5,4:T(8,128)} %constant_dynamic-slice_fusion.2) | copy-start | bytes 3145732
  158.8 13.5 %collective-permute-start.1 = (bf16[2,2,1,8,4,4,4,128]{7,6,5,4,3,2,1,0:T(4,128)(2,1)S(1)}, bf16[2,2,1,8,4,4,4,128]{7,6,5,4,3,2,1,0:T(4,128)(2,1)}, u32[]{:S(2)}, u32[]{:S(2)}) collective-permute-start(bf16[2,2,1,8,4,4,4,128]{7,6,5,4,3,2,1,0:T(4,128)(2,1)S(1)} %copy.358), channel_id=1, source_target_pairs={{0,1},{1,0},{2,3},{3,2},{4,5},{5,4},{6,7},{7,6},{8,9},{9,8},{10,11... | collective-permute-start | bytes 1572872 | tf_op jit(solution)/shard_map/ppermute | solution.py:130
  160.5 5.0 %collective-permute-start.2 = (f32[2,2,1,1,8,4,4,4]{4,7,6,5,3,2,1,0:T(4,128)S(1)}, f32[2,2,1,1,8,4,4,4]{4,7,6,5,3,2,1,0:T(4,128)S(1)}, u32[]{:S(2)}, u32[]{:S(2)}) collective-permute-start(f32[2,2,1,1,8,4,4,4]{4,7,6,5,3,2,1,0:T(4,128)S(1)} %get-tuple-element.49), channel_id=1, source_target_pairs={{0,2},{1,3},{2,0},{3,1},{4,6},{5,7},{6,4},{7,5},{8,10},{9,11},{10,... | collective-permute-start | bytes 24584 | tf_op jit(solution)/shard_map/ppermute | solution.py:129
  165.5 2.7 %copy-start.9 = (f32[2,2,1,1,8,4,4,4]{4,7,6,5,3,2,1,0:T(4,128)}, f32[2,2,1,1,8,4,4,4]{4,7,6,5,3,2,1,0:T(4,128)S(1)}, u32[]{:S(2)}) copy-start(f32[2,2,1,1,8,4,4,4]{4,7,6,5,3,2,1,0:T(4,128)S(1)} %collective-permute-done.2) | copy-start | bytes 24580
  165.6 11.4 %collective-permute-start.4 = (f32[2,1,1,1,8,4,4,4]{4,7,6,5,3,2,1,0:T(4,128)S(1)}, f32[2,1,1,1,8,4,4,4]{4,7,6,5,3,2,1,0:T(4,128)S(1)}, u32[]{:S(2)}, u32[]{:S(2)}) collective-permute-start(f32[2,1,1,1,8,4,4,4]{4,7,6,5,3,2,1,0:T(4,128)S(1)} %get-tuple-element.53), channel_id=1, source_target_pairs={{0,4},{1,5},{2,6},{3,7},{4,0},{5,1},{6,2},{7,3},{8,12},{9,13},{10,... | collective-permute-start | bytes 12296 | tf_op jit(solution)/shard_map/ppermute | solution.py:129
  172.3 4.2 %copy-start.10 = (f32[2,2,1,1,8,4,4,4]{4,7,6,5,3,2,1,0:T(4,128)S(1)}, f32[2,2,1,1,8,4,4,4]{4,7,6,5,3,2,1,0:T(4,128)}, u32[]{:S(2)}) copy-start(f32[2,2,1,1,8,4,4,4]{4,7,6,5,3,2,1,0:T(4,128)} %copy-done.9) | copy-start | bytes 24580
  174.8 10.1 %copy-start.12 = (f32[8,4,4,4]{0,3,2,1:T(4,128)S(1)}, f32[8,4,4,4]{0,3,2,1:T(4,128)}, u32[]{:S(2)}) copy-start(f32[8,4,4,4]{0,3,2,1:T(4,128)} %copy-done.11) | copy-start | bytes 6148
  174.8 10.1 %copy-start.14 = (f32[8,4,4,4]{0,3,2,1:T(4,128)S(1)}, f32[8,4,4,4]{0,3,2,1:T(4,128)}, u32[]{:S(2)}) copy-start(f32[8,4,4,4]{0,3,2,1:T(4,128)} %get-tuple-element.51) | copy-start | bytes 6148
  174.8 15.0 %copy-start.13 = (bf16[8,4,4,4,4]{4,3,2,1,0:T(4,128)(2,1)S(1)}, bf16[8,4,4,4,4]{4,3,2,1,0:T(4,128)(2,1)}, u32[]{:S(2)}) copy-start(bf16[8,4,4,4,4]{4,3,2,1,0:T(4,128)(2,1)} %copy.308) | copy-start | bytes 12292
  174.9 6.8 %collective-permute-start.3 = (bf16[2,1,1,8,4,4,4,128]{7,6,5,4,3,2,1,0:T(4,128)(2,1)S(1)}, bf16[2,1,1,8,4,4,4,128]{7,6,5,4,3,2,1,0:T(4,128)(2,1)S(1)}, u32[]{:S(2)}, u32[]{:S(2)}) collective-permute-start(bf16[2,1,1,8,4,4,4,128]{7,6,5,4,3,2,1,0:T(4,128)(2,1)S(1)} %dynamic-slice_convert_fusion.1), channel_id=1, source_target_pairs={{0,2},{1,3},{2,0},{3,1},{4,6},{5,7},{6,4},{7,5},{8,10},{9,11},{10,... | collective-permute-start | bytes 786440 | tf_op jit(solution)/shard_map/ppermute | solution.py:130
  182.4 7.3 %collective-permute-start.5 = (bf16[1,1,1,8,4,4,4,128]{7,6,5,4,3,2,1,0:T(4,128)(2,1)S(1)}, bf16[1,1,1,8,4,4,4,128]{7,6,5,4,3,2,1,0:T(4,128)(2,1)S(1)}, u32[]{:S(2)}, u32[]{:S(2)}) collective-permute-start(bf16[1,1,1,8,4,4,4,128]{7,6,5,4,3,2,1,0:T(4,128)(2,1)S(1)} %dynamic-slice_convert_fusion.2), channel_id=1, source_target_pairs={{0,4},{1,5},{2,6},{3,7},{4,0},{5,1},{6,2},{7,3},{8,12},{9,13},{10,... | collective-permute-start | bytes 393224 | tf_op jit(solution)/shard_map/ppermute | solution.py:130
  200.1 58.9 %copy-start.1 = (bf16[2560,512]{1,0:T(8,128)(2,1)S(1)}, bf16[2560,512]{1,0:T(8,128)(2,1)}, u32[]{:S(2)}) copy-start(bf16[2560,512]{1,0:T(8,128)(2,1)} %param.15) | copy-start | bytes 7864324
  200.1 55.5 %all-gather.6.cloned.1.call-start = ((), (), s32[]{:S(2)}) async-start(), calls=%async_computation.3 | async-start | bytes 1474560 | tf_op jit(solution)/shard_map/all_gather | solution.py:236
Sparse Core Ops, SparseCore 0:
  15.5 41.5 all-gather.3
  84.0 23.1 all-reduce.2
  200.3 11.4 reduce-scatter.1
  213.8 41.7 all-gather.5
where the time goes:
time: 267 us; the launch traced here: 266 us
  waiting for transfers between devices  108 us (40%)
  local copies, waits for them, and re-layouts  62.8 us (24%)
  matrix products  37.9 us (14%)
  other arithmetic  26.2 us (10%)
  between operations  14.9 us (6%)
  starting transfers between devices  10.7 us (4%)
  blocking collectives  4.57 us (2%)
    all_gather x1, waiting for transfers between devices, on_device(): gathered = lax.all_gather(normed, 'col', axis=0, tiled=True)  41.7 us
    all_gather x1, waiting for transfers between devices, on_device(): attended = lax.all_gather(own_out, 'seq', axis=0, tiled=True)  41 us
    dot_general x3, matrix products, on_device(): jnp.dot(piece_rows, matrix, preferred_element_type=jnp.float32)  13.4 us
    ppermute x3, waiting for transfers between devices, seq_merge(): lax.ppermute(send_values.astype(jnp.bfloat16), 'seq', pairs)  12.6 us
    reshape x1, local copies, waits for them, and re-layouts, on_device(): paged_value_cache.reshape(paged_value_cache.shape[0], block_len, heads_kv...  12.4 us
    reshape x1, local copies, waits for them, and re-layouts, on_device(): paged_key_cache.reshape(paged_key_cache.shape[0], block_len, heads_kv, HE...  12.4 us
    reduce_scatter x1, waiting for transfers between devices, on_device(): lax.psum_scatter(partials.astype(jnp.bfloat16), 'col', scatter_dimension=...  11.6 us
    dot_general x1, matrix products, slot_parts(): jnp.einsum('nsagh,nbah->nasgb', slot_queries, key_rows, preferred_element...  7.94 us
  transfers between devices with their start and end apart: 10, of which 7 were waited for; matrix products, arithmetic and copies ran while one was open for 18% of the time, Pallas kernels for 0%

commit v1 on v0

--- a/solution.py
+++ b/solution.py
@@ -233,7 +233,12 @@
     own_out = lax.psum_scatter(
         partials.astype(jnp.bfloat16), "col", scatter_dimension=0, tiled=True
     ).reshape(per, step_count, -1)
-    attended = lax.all_gather(own_out, "seq", axis=0, tiled=True)
+    ring = [own_out]
+    for hop in range(7):
+        ring.append(lax.ppermute(ring[-1], "seq", [(dev, (dev + 1) % 8) for dev in range(8)]))
+    attended = jnp.roll(
+        jnp.concatenate(ring[::-1], axis=0), (lax.axis_index("seq") + 1) * ring[0].shape[0], axis=0
+    )
     return (
         attended,
         current_key.reshape(req_count, step_count, k_width),

time: 267 us -> 283 us (1.060)
  waiting for transfers between devices: 108 us -> 122 us
    ppermute x0 -> x7, waiting for transfers between devices: none -> 54.3 us  [on_device(): lax.ppermute(ring[-1], 'seq', [(dev, (dev + 1) % 8) for dev in range(8)])]
    all_gather x1 -> x0, waiting for transfers between devices: 41 us -> none  [on_device(): attended = lax.all_gather(own_out, 'seq', axis=0, tiled=True)]
    unnamed x46 -> x57, local copies, waits for them, and re-layouts: 6.27 us -> 6.1 us
  transfers between devices with their start and end apart: 10 -> 16, of which waited for: 7 -> 13; matrix products, arithmetic and copies ran while one was open for 18% -> 17% of each run, Pallas kernels for 0% -> 0%
where the time goes in v1:
time: 283 us; the launch traced here: 281 us
  waiting for transfers between devices  122 us (43%)
  local copies, waits for them, and re-layouts  64.3 us (23%)
  matrix products  37.9 us (13%)
  other arithmetic  25.5 us (9%)
  between operations  15 us (5%)
  starting transfers between devices  12.1 us (4%)
  blocking collectives  4.57 us (2%)
    ppermute x7, waiting for transfers between devices, on_device(): lax.ppermute(ring[-1], 'seq', [(dev, (dev + 1) % 8) for dev in range(8)])  54.3 us
    all_gather x1, waiting for transfers between devices, on_device(): gathered = lax.all_gather(normed, 'col', axis=0, tiled=True)  41.7 us
    dot_general x3, matrix products, on_device(): jnp.dot(piece_rows, matrix, preferred_element_type=jnp.float32)  13.4 us
    ppermute x3, waiting for transfers between devices, seq_merge(): lax.ppermute(send_values.astype(jnp.bfloat16), 'seq', pairs)  12.6 us
    reshape x1, local copies, waits for them, and re-layouts, on_device(): paged_value_cache.reshape(paged_value_cache.shape[0], block_len, heads_kv...  12.4 us
    reshape x1, local copies, waits for them, and re-layouts, on_device(): paged_key_cache.reshape(paged_key_cache.shape[0], block_len, heads_kv, HE...  12.4 us
    reduce_scatter x1, waiting for transfers between devices, on_device(): lax.psum_scatter(partials.astype(jnp.bfloat16), 'col', scatter_dimension=...  11.6 us
    dot_general x1, matrix products, slot_parts(): jnp.einsum('nsagh,nbah->nasgb', slot_queries, key_rows, preferred_element...  7.95 us
  transfers between devices with their start and end apart: 16, of which 13 were waited for; matrix products, arithmetic and copies ran while one was open for 17% of the time, Pallas kernels for 0%

profile of v1, /device:TPU:0, one launch (start us, length us, event | category | flops | bytes accessed | tf_op | source)
XLA Modules:
  0.0 281.3 jit_solution(17020094624939860004)
XLA Ops:
  7.2 2.2 fusion.9
  9.5 2.6 psum.7
  12.2 3.1 %fusion.11 = bf16[64,4,2560]{2,1,0:T(4,128)(2,1)} fusion(bf16[64,4,2560]{2,1,0:T(4,128)(2,1)} %param.11, f32[2560]{0:T(1024)} %param.12, f32[64,4]{1,0:T(8,128)S(1)} %copy.273), kind=kLoop, calls=%fused_computation.16 | loop fusion | flops 2621440 | bytes 2632704 | tf_op jit(solution)/shard_map/convert_element_type | solution.py:168
  15.4 41.7 %all-gather.2.cloned.1.call-done = bf16[128,4,2560]{2,1,0:T(4,128)(2,1)} async-done(((bf16[64,4,2560]{2,1,0:T(4,128)(2,1)}), bf16[128,4,2560]{2,1,0:T(4,128)(2,1)}) %all-gather.2.cloned.1.call-update) | async-done | bytes 2621456 | tf_op jit(solution)/shard_map/all_gather | solution.py:171
  57.1 5.3 %reshape.465 = bf16[512,2560]{1,0:T(8,128)(2,1)} reshape(bf16[128,4,2560]{2,1,0:T(4,128)(2,1)} %all-gather.2.cloned.1.call-done) | data formatting | bytes 5242880 | tf_op jit(solution)/shard_map/reshape | solution.py:172
  62.5 3.4 %convolution_convert_fusion.1 = bf16[512,512]{1,0:T(8,128)(2,1)S(1)} fusion(bf16[512,2560]{1,0:T(8,128)(2,1)} %reshape.465, bf16[2560,512]{1,0:T(8,128)(2,1)S(1)} %copy-done), kind=kOutput, calls=%fused_computation.26 | convolution fusion | flops 1342439424 | bytes 5767168 | tf_op jit(solution)/shard_map/dot_general | solution.py:174
  65.9 1.5 convolution_convert_fusion.2
  67.4 8.5 %convolution_convert_fusion = bf16[512,2048]{1,0:T(8,128)(2,1)S(1)} fusion(bf16[512,2560]{1,0:T(8,128)(2,1)S(1)} %copy-done.5, bf16[2560,2048]{1,0:T(8,128)(2,1)} %param.13), kind=kOutput, calls=%fused_computation.13 | convolution fusion | flops 5369757696 | bytes 15204352 | tf_op jit(solution)/shard_map/dot_general | solution.py:174
  75.9 1.8 pad_maximum_fusion
  77.7 6.1 %convert_element_type.83 = bf16[128,4,3072]{2,1,0:T(4,128)(2,1)} reshape(bf16[512,3072]{1,0:T(8,128)(2,1)} %pad_maximum_fusion) | data formatting | bytes 6291456 | tf_op jit(solution)/shard_map/convert_element_type | solution.py:179
  84.5 0.8 gather_fusion
  85.4 1.1 multiply_cosine_fusion
  86.5 12.4 %reshape.467 = bf16[50,128,4,128]{3,2,1,0:T(4,128)(2,1)} reshape(bf16[50,128,512]{2,1,0:T(8,128)(2,1)} %param.20) | data formatting | bytes 13107200 | tf_op jit(solution)/shard_map/reshape | solution.py:161
  98.9 12.4 %reshape.468 = bf16[50,128,4,128]{3,2,1,0:T(4,128)(2,1)} reshape(bf16[50,128,512]{2,1,0:T(8,128)(2,1)} %param.21) | data formatting | bytes 13107200 | tf_op jit(solution)/shard_map/reshape | solution.py:162
  113.0 1.8 dynamic-slice_convert_fusion
  114.8 0.9 slice_bitcast_fusion.2
  115.8 0.8 copy-done.3
  116.6 1.5 slice.92
  118.1 2.3 reshape.508
  120.4 0.7 fusion.76
  121.8 1.4 pad_maximum_fusion.1
  123.8 2.2 gather_fusion.1
  125.9 8.0 %select_reduce_fusion.1 = (f32[50,4,4,4]{3,2,1,0:T(4,128)S(1)}, f32[50,4,4,4,128]{4,3,2,1,0:T(4,128)}) fusion(pred[50,4,128]{2,1,0:T(4,128)(4,1)S(1)} %or_and_fusion, bf16[50,4,4,4,128]{4,3,1,2,0:T(4,128)(2,1)} %gather_fusion.1, bf16[50,128,4,128,1]{3,2,1,0,4:T(4,128)(2,1)} %bitcast.125), kind=kOutput, calls=%fused_computation.23 | convolution fusion | flops 106083200 | bytes 9049600 | tf_op jit(solution)/shard_map/nsagh,nbah->nasgb/dot_general | solution.py:37
  133.9 1.3 select_reduce_fusion
  135.1 1.1 stack.10
  137.5 1.2 fusion.36
  139.4 0.8 fusion.40
  140.2 1.7 copy_dynamic-update-slice_fusion.1
  141.9 3.2 %fusion.18 = f32[50,4,4,4]{3,2,1,0:T(4,128)S(1)} fusion(f32[50,4,4,4,128]{4,3,2,1,0:T(4,128)} %get-tuple-element.60, f32[50,4,4,4]{3,2,1,0:T(4,128)S(1)} %get-tuple-element.59, pred[50,4,128]{2,1,0:T(4,128)(4,1)S(1)} %or_and_fusion), kind=kLoop, calls=%fused_computation.33 | loop fusion | flops 1635200 | bytes 1689600 | tf_op jit(solution)/shard_map/reduce_sum | solution.py:53
  145.1 0.8 gather_fusion.2
  147.0 0.8 copy_dynamic-update-slice_fusion
  147.7 1.7 constant_dynamic-slice_fusion.2
  149.4 1.6 collective-permute-start
  151.0 4.7 %fusion.14 = f32[50,4,4,4,128]{4,3,2,1,0:T(4,128)S(1)} fusion(bf16[50,128,4,128,1]{3,2,1,0,4:T(4,128)(2,1)} %bitcast.124, f32[50,4,4,4,128]{4,3,2,1,0:T(4,128)} %get-tuple-element.60, f32[50,4,4,4]{3,2,1,0:T(4,128)S(1)} %bitcast.137, f32[50,4,4,4]{3,2,1,0:T(4,128)S(1)} %get-tuple-element.59, pred[50,4,128]{2,1,0:T(4,128)(4,1)S(1)} %copy-done.14), kind=kOutput, calls=%fused_computation.25 | convolution fusion | flops 106905600 | bytes 9881600 | tf_op jit(solution)/shard_map/nasgb,nbah->nasgh/dot_general | solution.py:54
  155.8 2.2 fusion.12
  157.9 1.1 constant_dynamic-slice_fusion.3
  159.2 1.1 copy.308
  161.1 1.1 fusion.33
  162.3 1.6 collective-permute-start.2
  163.9 1.0 fusion.28
  165.8 1.5 collective-permute-done.2
  167.4 2.6 collective-permute-start.4
  170.0 4.1 %collective-permute-done.1 = bf16[2,2,1,8,4,4,4,128]{7,6,5,4,3,2,1,0:T(4,128)(2,1)} collective-permute-done((bf16[2,2,1,8,4,4,4,128]{7,6,5,4,3,2,1,0:T(4,128)(2,1)S(1)}, bf16[2,2,1,8,4,4,4,128]{7,6,5,4,3,2,1,0:T(4,128)(2,1)}, u32[]{:S(2)}, u32[]{:S(2)}) %collective-permute-start.1) | collective-permute-done | bytes 524320 | tf_op jit(solution)/shard_map/ppermute | solution.py:130
  174.1 2.5 fusion.17
  176.7 1.6 collective-permute-start.3
  178.9 4.7 %collective-permute-done.3 = bf16[2,1,1,8,4,4,4,128]{7,6,5,4,3,2,1,0:T(4,128)(2,1)S(1)} collective-permute-done((bf16[2,1,1,8,4,4,4,128]{7,6,5,4,3,2,1,0:T(4,128)(2,1)S(1)}, bf16[2,1,1,8,4,4,4,128]{7,6,5,4,3,2,1,0:T(4,128)(2,1)S(1)}, u32[]{:S(2)}, u32[]{:S(2)}) %collective-permute-start.3) | collective-permute-done | bytes 262176 | tf_op jit(solution)/shard_map/ppermute | solution.py:130
  183.5 0.6 multiply_add_fusion.1
  184.2 2.5 collective-permute-start.5
  187.6 3.9 %collective-permute-done.5 = bf16[1,1,1,8,4,4,4,128]{7,6,5,4,3,2,1,0:T(4,128)(2,1)S(1)} collective-permute-done((bf16[1,1,1,8,4,4,4,128]{7,6,5,4,3,2,1,0:T(4,128)(2,1)S(1)}, bf16[1,1,1,8,4,4,4,128]{7,6,5,4,3,2,1,0:T(4,128)(2,1)S(1)}, u32[]{:S(2)}, u32[]{:S(2)}) %collective-permute-start.5) | collective-permute-done | bytes 131104 | tf_op jit(solution)/shard_map/ppermute | solution.py:130
  191.5 1.6 fusion.38
  193.3 2.0 all_gather.8
  195.3 6.6 %fusion.6 = bf16[2,8,4,2560]{3,1,2,0:T(8,128)(2,1)} fusion(bf16[2,8,4,2048]{3,1,2,0:T(8,128)(2,1)S(1)} %all_gather.8, bf16[2048,2560]{1,0:T(8,128)(2,1)} %param.16), kind=kOutput, calls=%fused_computation.9 | convolution fusion | flops 671252480 | bytes 11075584 | tf_op jit(solution)/shard_map/dot_general | solution.py:229
  201.9 11.6 %reduce-scatter.2.cloned.1.call-done = bf16[1,8,4,2560]{3,1,2,0:T(8,128)(2,1)} async-done(((bf16[2,8,4,2560]{3,1,2,0:T(8,128)(2,1)}), bf16[1,8,4,2560]{3,1,2,0:T(8,128)(2,1)}) %reduce-scatter.2.cloned.1.call-update) | async-done | bytes 163856 | tf_op jit(solution)/shard_map/reduce_scatter | solution.py:233
  213.6 1.5 collective-permute-start.6
  215.0 7.4 %collective-permute-done.6 = bf16[8,4,2560]{2,0,1:T(8,128)(2,1)S(1)} collective-permute-done((bf16[8,4,2560]{2,0,1:T(8,128)(2,1)}, bf16[8,4,2560]{2,0,1:T(8,128)(2,1)S(1)}, u32[]{:S(2)}, u32[]{:S(2)}) %collective-permute-start.6) | collective-permute-done | bytes 163872 | tf_op jit(solution)/shard_map/ppermute | solution.py:238
  222.4 8.0 %collective-permute-done.7 = bf16[8,4,2560]{2,0,1:T(8,128)(2,1)S(1)} collective-permute-done((bf16[8,4,2560]{2,0,1:T(8,128)(2,1)S(1)}, bf16[8,4,2560]{2,0,1:T(8,128)(2,1)S(1)}, u32[]{:S(2)}, u32[]{:S(2)}) %collective-permute-start.7) | collective-permute-done | bytes 163872 | tf_op jit(solution)/shard_map/ppermute | solution.py:238
  230.4 8.0 %collective-permute-done.8 = bf16[8,4,2560]{2,0,1:T(8,128)(2,1)S(1)} collective-permute-done((bf16[8,4,2560]{2,0,1:T(8,128)(2,1)S(1)}, bf16[8,4,2560]{2,0,1:T(8,128)(2,1)S(1)}, u32[]{:S(2)}, u32[]{:S(2)}) %collective-permute-start.8) | collective-permute-done | bytes 163872 | tf_op jit(solution)/shard_map/ppermute | solution.py:238
  238.4 8.0 %collective-permute-done.9 = bf16[8,4,2560]{2,0,1:T(8,128)(2,1)S(1)} collective-permute-done((bf16[8,4,2560]{2,0,1:T(8,128)(2,1)S(1)}, bf16[8,4,2560]{2,0,1:T(8,128)(2,1)S(1)}, u32[]{:S(2)}, u32[]{:S(2)}) %collective-permute-start.9) | collective-permute-done | bytes 163872 | tf_op jit(solution)/shard_map/ppermute | solution.py:238
  246.5 8.3 %collective-permute-done.10 = bf16[8,4,2560]{2,0,1:T(8,128)(2,1)S(1)} collective-permute-done((bf16[8,4,2560]{2,0,1:T(8,128)(2,1)S(1)}, bf16[8,4,2560]{2,0,1:T(8,128)(2,1)S(1)}, u32[]{:S(2)}, u32[]{:S(2)}) %collective-permute-start.10) | collective-permute-done | bytes 163872 | tf_op jit(solution)/shard_map/ppermute | solution.py:238
  254.8 9.4 %collective-permute-done.11 = bf16[8,4,2560]{2,0,1:T(8,128)(2,1)S(1)} collective-permute-done((bf16[8,4,2560]{2,0,1:T(8,128)(2,1)S(1)}, bf16[8,4,2560]{2,0,1:T(8,128)(2,1)S(1)}, u32[]{:S(2)}, u32[]{:S(2)}) %collective-permute-start.11) | collective-permute-done | bytes 163872 | tf_op jit(solution)/shard_map/ppermute | solution.py:238
  264.2 1.8 slice.146
  266.0 1.1 fusion.87
  267.1 5.1 %collective-permute-done.12 = bf16[8,4,2560]{2,0,1:T(8,128)(2,1)S(1)} collective-permute-done((bf16[8,4,2560]{2,0,1:T(8,128)(2,1)S(1)}, bf16[8,4,2560]{2,0,1:T(8,128)(2,1)S(1)}, u32[]{:S(2)}, u32[]{:S(2)}) %collective-permute-start.12) | collective-permute-done | bytes 163872 | tf_op jit(solution)/shard_map/ppermute | solution.py:238
  272.7 2.1 copy.315
  (121 shorter events, 10.4 us)
Async XLA Ops:
  7.2 55.3 %copy-start = (bf16[2560,512]{1,0:T(8,128)(2,1)S(1)}, bf16[2560,512]{1,0:T(8,128)(2,1)}, u32[]{:S(2)}) copy-start(bf16[2560,512]{1,0:T(8,128)(2,1)} %param.15) | copy-start | bytes 7864324
  7.2 50.0 %all-gather.2.cloned.1.call-start = ((), (), s32[]{:S(2)}) async-start(), calls=%async_computation.1 | async-start | bytes 3932160 | tf_op jit(solution)/shard_map/all_gather | solution.py:171
  15.4 97.6 %all-reduce.3.cloned.1.call-start = ((), (), s32[]{:S(2)}) async-start(), calls=%async_computation.3 | async-start | bytes 6291456
  62.5 3.4 %copy-start.5 = (bf16[512,2560]{1,0:T(8,128)(2,1)S(1)}, bf16[512,2560]{1,0:T(8,128)(2,1)}, u32[]{:S(2)}) copy-start(bf16[512,2560]{1,0:T(8,128)(2,1)} %reshape.465) | copy-start | bytes 7864324
  62.5 3.4 %copy-start.16 = (bf16[2560,512]{1,0:T(8,128)(2,1)S(1)}, bf16[2560,512]{1,0:T(8,128)(2,1)}, u32[]{:S(2)}) copy-start(bf16[2560,512]{1,0:T(8,128)(2,1)} %param.14) | copy-start | bytes 7864324
  83.8 0.7 copy-start.15
  83.8 0.7 copy-start.2
  83.8 129.7 %reduce-scatter.2.cloned.1.call-start = ((), (), s32[]{:S(2)}) async-start(), calls=%async_computation.2 | async-start | bytes 491520 | tf_op jit(solution)/shard_map/reduce_scatter | solution.py:233
  98.9 12.4 %copy-start.18 = (u32[32]{0:T(128)S(1)}, u32[32]{0:T(128)}, u32[]{:S(2)}) copy-start(u32[32]{0:T(128)} %constant.111) | copy-start | bytes 388
  98.9 13.6 %copy-start.17 = (s32[50]{0:T(128)S(1)}, s32[50]{0:T(128)}, u32[]{:S(2)}) copy-start(s32[50]{0:T(128)} %param.19) | copy-start | bytes 604
  113.0 29.0 %copy-start.13 = (pred[50,4,128]{2,1,0:T(4,128)(4,1)}, pred[50,4,128]{2,1,0:T(4,128)(4,1)S(1)}, u32[]{:S(2)}) copy-start(pred[50,4,128]{2,1,0:T(4,128)(4,1)S(1)} %or_and_fusion) | copy-start | bytes 76804
  114.8 1.7 copy-start.3
  139.4 2.6 copy-start.9
  145.1 5.9 %copy-start.14 = (pred[50,4,128]{2,1,0:T(4,128)(4,1)S(1)}, pred[50,4,128]{2,1,0:T(4,128)(4,1)}, u32[]{:S(2)}) copy-start(pred[50,4,128]{2,1,0:T(4,128)(4,1)} %copy-done.13) | copy-start | bytes 76804
  149.4 11.7 %collective-permute-start = (f32[2,2,2,1,8,4,4,4]{4,7,6,5,2,1,3,0:T(4,128)}, f32[2,2,2,1,8,4,4,4]{4,7,6,5,2,1,3,0:T(4,128)S(1)}, u32[]{:S(2)}, u32[]{:S(2)}) collective-permute-start(f32[2,2,2,1,8,4,4,4]{4,7,6,5,2,1,3,0:T(4,128)} %constant_dynamic-slice_fusion.2), channel_id=1, source_target_pairs={{0,1},{1,0},{2,3},{3,2},{4,5},{5,4},{6,7},{7,6},{8,9},{9,8},{10,11... | collective-permute-start | bytes 49160 | tf_op jit(solution)/shard_map/ppermute | solution.py:129
  159.2 14.9 %copy-start.4 = (f32[2,2,1,8,4,4,4,128]{7,3,2,1,0,6,5,4:T(8,128)S(1)}, f32[2,2,1,8,4,4,4,128]{7,3,2,1,0,6,5,4:T(8,128)}, u32[]{:S(2)}) copy-start(f32[2,2,1,8,4,4,4,128]{7,3,2,1,0,6,5,4:T(8,128)} %constant_dynamic-slice_fusion.3) | copy-start | bytes 3145732
  160.6 13.5 %collective-permute-start.1 = (bf16[2,2,1,8,4,4,4,128]{7,6,5,4,3,2,1,0:T(4,128)(2,1)S(1)}, bf16[2,2,1,8,4,4,4,128]{7,6,5,4,3,2,1,0:T(4,128)(2,1)}, u32[]{:S(2)}, u32[]{:S(2)}) collective-permute-start(bf16[2,2,1,8,4,4,4,128]{7,6,5,4,3,2,1,0:T(4,128)(2,1)S(1)} %copy.358), channel_id=1, source_target_pairs={{0,1},{1,0},{2,3},{3,2},{4,5},{5,4},{6,7},{7,6},{8,9},{9,8},{10,11... | collective-permute-start | bytes 1572872 | tf_op jit(solution)/shard_map/ppermute | solution.py:130
  162.3 5.0 %collective-permute-start.2 = (f32[2,2,1,1,8,4,4,4]{4,7,6,5,3,2,1,0:T(4,128)S(1)}, f32[2,2,1,1,8,4,4,4]{4,7,6,5,3,2,1,0:T(4,128)S(1)}, u32[]{:S(2)}, u32[]{:S(2)}) collective-permute-start(f32[2,2,1,1,8,4,4,4]{4,7,6,5,3,2,1,0:T(4,128)S(1)} %get-tuple-element.49), channel_id=1, source_target_pairs={{0,2},{1,3},{2,0},{3,1},{4,6},{5,7},{6,4},{7,5},{8,10},{9,11},{10,... | collective-permute-start | bytes 24584 | tf_op jit(solution)/shard_map/ppermute | solution.py:129
  167.3 2.7 copy-start.7
  167.4 19.3 %copy-start.10 = (f32[8,4,4,4]{0,3,2,1:T(4,128)S(1)}, f32[8,4,4,4]{0,3,2,1:T(4,128)}, u32[]{:S(2)}) copy-start(f32[8,4,4,4]{0,3,2,1:T(4,128)} %copy-done.9) | copy-start | bytes 6148
  167.4 19.2 %copy-start.12 = (f32[8,4,4,4]{0,3,2,1:T(4,128)S(1)}, f32[8,4,4,4]{0,3,2,1:T(4,128)}, u32[]{:S(2)}) copy-start(f32[8,4,4,4]{0,3,2,1:T(4,128)} %get-tuple-element.51) | copy-start | bytes 6148
  167.4 11.4 %collective-permute-start.4 = (f32[2,1,1,1,8,4,4,4]{4,7,6,5,3,2,1,0:T(4,128)S(1)}, f32[2,1,1,1,8,4,4,4]{4,7,6,5,3,2,1,0:T(4,128)S(1)}, u32[]{:S(2)}, u32[]{:S(2)}) collective-permute-start(f32[2,1,1,1,8,4,4,4]{4,7,6,5,3,2,1,0:T(4,128)S(1)} %get-tuple-element.53), channel_id=1, source_target_pairs={{0,4},{1,5},{2,6},{3,7},{4,0},{5,1},{6,2},{7,3},{8,12},{9,13},{10,... | collective-permute-start | bytes 12296 | tf_op jit(solution)/shard_map/ppermute | solution.py:129
  174.1 4.2 %copy-start.8 = (f32[2,2,1,1,8,4,4,4]{4,7,6,5,3,2,1,0:T(4,128)S(1)}, f32[2,2,1,1,8,4,4,4]{4,7,6,5,3,2,1,0:T(4,128)}, u32[]{:S(2)}) copy-start(f32[2,2,1,1,8,4,4,4]{4,7,6,5,3,2,1,0:T(4,128)} %copy-done.7) | copy-start | bytes 24580
  176.6 15.0 %copy-start.11 = (bf16[8,4,4,4,4]{4,3,2,1,0:T(4,128)(2,1)S(1)}, bf16[8,4,4,4,4]{4,3,2,1,0:T(4,128)(2,1)}, u32[]{:S(2)}) copy-start(bf16[8,4,4,4,4]{4,3,2,1,0:T(4,128)(2,1)} %copy.308) | copy-start | bytes 12292
  176.7 6.8 %collective-permute-start.3 = (bf16[2,1,1,8,4,4,4,128]{7,6,5,4,3,2,1,0:T(4,128)(2,1)S(1)}, bf16[2,1,1,8,4,4,4,128]{7,6,5,4,3,2,1,0:T(4,128)(2,1)S(1)}, u32[]{:S(2)}, u32[]{:S(2)}) collective-permute-start(bf16[2,1,1,8,4,4,4,128]{7,6,5,4,3,2,1,0:T(4,128)(2,1)S(1)} %dynamic-slice_convert_fusion.1), channel_id=1, source_target_pairs={{0,2},{1,3},{2,0},{3,1},{4,6},{5,7},{6,4},{7,5},{8,10},{9,11},{10,... | collective-permute-start | bytes 786440 | tf_op jit(solution)/shard_map/ppermute | solution.py:130
  184.2 7.3 %collective-permute-start.5 = (bf16[1,1,1,8,4,4,4,128]{7,6,5,4,3,2,1,0:T(4,128)(2,1)S(1)}, bf16[1,1,1,8,4,4,4,128]{7,6,5,4,3,2,1,0:T(4,128)(2,1)S(1)}, u32[]{:S(2)}, u32[]{:S(2)}) collective-permute-start(bf16[1,1,1,8,4,4,4,128]{7,6,5,4,3,2,1,0:T(4,128)(2,1)S(1)} %dynamic-slice_convert_fusion.2), channel_id=1, source_target_pairs={{0,4},{1,5},{2,6},{3,7},{4,0},{5,1},{6,2},{7,3},{8,12},{9,13},{10,... | collective-permute-start | bytes 393224 | tf_op jit(solution)/shard_map/ppermute | solution.py:130
  213.6 58.8 %copy-start.6 = (bf16[1,8,4,2560]{3,1,2,0:T(8,128)(2,1)S(1)}, bf16[1,8,4,2560]{3,1,2,0:T(8,128)(2,1)}, u32[]{:S(2)}) copy-start(bf16[1,8,4,2560]{3,1,2,0:T(8,128)(2,1)} %reduce-scatter.2.cloned.1.call-done) | copy-start | bytes 491524
  213.6 8.9 %collective-permute-start.6 = (bf16[8,4,2560]{2,0,1:T(8,128)(2,1)}, bf16[8,4,2560]{2,0,1:T(8,128)(2,1)S(1)}, u32[]{:S(2)}, u32[]{:S(2)}) collective-permute-start(bf16[8,4,2560]{2,0,1:T(8,128)(2,1)} %bitcast.134), channel_id=1, source_target_pairs={{0,1},{1,2},{2,3},{3,4},{4,5},{5,6},{6,7},{7,0},{8,9},{9,10},{10,1... | collective-permute-start | bytes 491528 | tf_op jit(solution)/shard_map/ppermute | solution.py:238
  222.4 8.0 %collective-permute-start.7 = (bf16[8,4,2560]{2,0,1:T(8,128)(2,1)S(1)}, bf16[8,4,2560]{2,0,1:T(8,128)(2,1)S(1)}, u32[]{:S(2)}, u32[]{:S(2)}) collective-permute-start(bf16[8,4,2560]{2,0,1:T(8,128)(2,1)S(1)} %collective-permute-done.6), channel_id=1, source_target_pairs={{0,1},{1,2},{2,3},{3,4},{4,5},{5,6},{6,7},{7,0},{8,9},{9,10},{10,1... | collective-permute-start | bytes 491528 | tf_op jit(solution)/shard_map/ppermute | solution.py:238
  230.4 8.0 %collective-permute-start.8 = (bf16[8,4,2560]{2,0,1:T(8,128)(2,1)S(1)}, bf16[8,4,2560]{2,0,1:T(8,128)(2,1)S(1)}, u32[]{:S(2)}, u32[]{:S(2)}) collective-permute-start(bf16[8,4,2560]{2,0,1:T(8,128)(2,1)S(1)} %collective-permute-done.7), channel_id=1, source_target_pairs={{0,1},{1,2},{2,3},{3,4},{4,5},{5,6},{6,7},{7,0},{8,9},{9,10},{10,1... | collective-permute-start | bytes 491528 | tf_op jit(solution)/shard_map/ppermute | solution.py:238
  238.4 8.0 %collective-permute-start.9 = (bf16[8,4,2560]{2,0,1:T(8,128)(2,1)S(1)}, bf16[8,4,2560]{2,0,1:T(8,128)(2,1)S(1)}, u32[]{:S(2)}, u32[]{:S(2)}) collective-permute-start(bf16[8,4,2560]{2,0,1:T(8,128)(2,1)S(1)} %collective-permute-done.8), channel_id=1, source_target_pairs={{0,1},{1,2},{2,3},{3,4},{4,5},{5,6},{6,7},{7,0},{8,9},{9,10},{10,1... | collective-permute-start | bytes 491528 | tf_op jit(solution)/shard_map/ppermute | solution.py:238
  246.5 8.3 %collective-permute-start.10 = (bf16[8,4,2560]{2,0,1:T(8,128)(2,1)S(1)}, bf16[8,4,2560]{2,0,1:T(8,128)(2,1)S(1)}, u32[]{:S(2)}, u32[]{:S(2)}) collective-permute-start(bf16[8,4,2560]{2,0,1:T(8,128)(2,1)S(1)} %collective-permute-done.9), channel_id=1, source_target_pairs={{0,1},{1,2},{2,3},{3,4},{4,5},{5,6},{6,7},{7,0},{8,9},{9,10},{10,1... | collective-permute-start | bytes 491528 | tf_op jit(solution)/shard_map/ppermute | solution.py:238
  254.8 9.4 %collective-permute-start.11 = (bf16[8,4,2560]{2,0,1:T(8,128)(2,1)S(1)}, bf16[8,4,2560]{2,0,1:T(8,128)(2,1)S(1)}, u32[]{:S(2)}, u32[]{:S(2)}) collective-permute-start(bf16[8,4,2560]{2,0,1:T(8,128)(2,1)S(1)} %collective-permute-done.10), channel_id=1, source_target_pairs={{0,1},{1,2},{2,3},{3,4},{4,5},{5,6},{6,7},{7,0},{8,9},{9,10},{10,1... | collective-permute-start | bytes 491528 | tf_op jit(solution)/shard_map/ppermute | solution.py:238
  264.2 8.0 %collective-permute-start.12 = (bf16[8,4,2560]{2,0,1:T(8,128)(2,1)S(1)}, bf16[8,4,2560]{2,0,1:T(8,128)(2,1)S(1)}, u32[]{:S(2)}, u32[]{:S(2)}) collective-permute-start(bf16[8,4,2560]{2,0,1:T(8,128)(2,1)S(1)} %collective-permute-done.11), channel_id=1, source_target_pairs={{0,1},{1,2},{2,3},{3,4},{4,5},{5,6},{6,7},{7,0},{8,9},{9,10},{10,1... | collective-permute-start | bytes 491528 | tf_op jit(solution)/shard_map/ppermute | solution.py:238
  272.5 2.2 copy-start.1
Sparse Core Ops, SparseCore 0:
  15.5 41.5 all-gather.1
  84.0 23.2 all-reduce.2
  202.1 11.4 reduce-scatter.1
